TPU v7x, 512 devices: a whole 4x8x8 slice. The times are simulated.
512 devices in a mesh: seq: 64 (over y, x, core), ch: 8 (over z).
Axes of the slice: x: 4, y: 8, z: 8, core: 2. Of those that a mesh axis runs over, the one named last changes fastest.
Arguments:
- signal: bfloat16 [1536, 32768], P('ch', 'seq'), may hold values from -16 to 16
- input_norm_gain: float32 [1536], P('ch'), may hold values from 0.25 to 1.75
- value_weight: bfloat16 [1536, 1536], P('seq', 'ch'), may hold values from -0.15625 to 0.15625
- gate_weight: bfloat16 [1536, 1536], P('seq', 'ch'), may hold values from -0.15625 to 0.15625
- depth_taps: float32 [31, 1536], P(None, 'ch'), may hold values from -1 to 1
- cotangent: bfloat16 [1536, 32768], P('ch', 'seq'), may hold values from -6 to 6
Outputs:
- output: bfloat16 [1536, 32768], P('ch', 'seq')
- signal_gradient: bfloat16 [1536, 32768], P('ch', 'seq')
- grad_value: float32 [1536, 1536], P('seq', 'ch')
- grad_gate: float32 [1536, 1536], P('seq', 'ch')
- grad_taps: float32 [31, 1536], P(None, 'ch')
- gain_gradient: float32 [1536], P('ch')
All inputs are finite; a program needn't handle non-finite values.
Results may differ from a plain program's by a relative error of at most 0.02.
Values may be sent and summed in bfloat16 or wider, within the bound.
No kernel may reach another device: no remote copies, remote signals or barrier semaphores. Data moves between devices by JAX's collectives and lax.ppermute only.
A program may use at most 64 MiB of HBM per device.

v0:
```python
import jax
import jax.numpy as jnp
from jax import lax
from jax.sharding import PartitionSpec as P


def extended(cells, sides, width):
    for axis, dim in sides:
        count = lax.axis_size(axis)
        ends = count - 1
        head = lax.slice_in_dim(cells, 0, width, axis=dim)
        tail = lax.slice_in_dim(cells, cells.shape[dim] - width, cells.shape[dim], axis=dim)
        cells = jnp.concatenate(
            [
                lax.ppermute(tail, axis, [(i, (i + 1) % count) for i in range(ends)]),
                cells,
                lax.ppermute(head, axis, [((i + 1) % count, i) for i in range(ends)]),
            ],
            axis=dim,
        )
    return cells


def standardize_rows(columns_in):
    values = columns_in.astype(jnp.float32)
    average = jnp.mean(values, 0, keepdims=True)
    centred = values - average
    spread = jnp.mean(centred * centred, 0, keepdims=True)
    inverse_deviation = lax.rsqrt(spread + 1e-05)
    return (centred * inverse_deviation, inverse_deviation)


def depthwise(padded, kernel):
    channels = padded.shape[0]
    result = lax.conv_general_dilated(
        padded[None],
        kernel,
        (1,),
        "VALID",
        dimension_numbers=("NCH", "OIH", "NCH"),
        feature_group_count=channels,
        precision=lax.Precision.HIGHEST,
    )
    return result[0]


def shards(signal, input_norm_gain, value_weight, gate_weight, depth_taps, cotangent):
    local_cols = signal.shape[0]
    frames = signal.shape[1]
    groups = lax.axis_size("ch")
    block_of_rows = frames // groups
    channel_position = lax.axis_index("ch")
    reach = depth_taps.shape[0] // 2
    complete_signal, complete_gain = (
        lax.all_gather(signal, "ch", axis=0, tiled=True),
        lax.all_gather(input_norm_gain.astype(jnp.bfloat16), "ch", axis=0, tiled=True).astype(
            input_norm_gain.dtype
        ),
    )
    centered_unit, inverse_deviation = standardize_rows(complete_signal)
    normalized_signal = (centered_unit * complete_gain[:, None]).astype(jnp.bfloat16)
    centered_unit_rows = lax.dynamic_slice_in_dim(
        centered_unit, channel_position * block_of_rows, block_of_rows, 1
    )
    row_inverse_deviation = lax.dynamic_slice_in_dim(
        inverse_deviation, channel_position * block_of_rows, block_of_rows, 1
    )
    stacked = jnp.concatenate([value_weight, gate_weight], 1)
    gathered = lax.all_gather(stacked, "seq", axis=0, tiled=True)
    mixed = lax.dot_general(
        gathered, normalized_signal, (((0,), (0,)), ((), ())), preferred_element_type=jnp.float32
    )
    value = mixed[:local_cols]
    gate = mixed[local_cols:]
    sig_gate = jax.nn.sigmoid(gate)
    glued = (value * sig_gate).astype(jnp.bfloat16)
    glued_pad = extended(glued, (("seq", 1),), reach).astype(jnp.float32)
    forward_kernel = depth_taps.T[:, None, :]
    pre = depthwise(glued_pad, forward_kernel)
    sig_pre = jax.nn.sigmoid(pre)
    output = (pre * sig_pre).astype(jnp.bfloat16)
    grad_pre = (cotangent.astype(jnp.float32) * sig_pre * (1.0 + pre * (1.0 - sig_pre))).astype(
        jnp.bfloat16
    )
    grad_pre_f = grad_pre.astype(jnp.float32)
    grad_pad = extended(grad_pre, (("seq", 1),), reach).astype(jnp.float32)
    grad_glued = depthwise(grad_pad, forward_kernel[:, :, ::-1])
    tap_partial = depthwise(glued_pad, grad_pre_f[:, None, :]).T
    grad_taps = lax.psum(tap_partial, "seq")
    grad_v = (grad_glued * sig_gate).astype(jnp.bfloat16)
    grad_g = (grad_glued * value * sig_gate * (1.0 - sig_gate)).astype(jnp.bfloat16)
    grad_both = jnp.concatenate([grad_v, grad_g], 0)
    weight_sums = lax.psum_scatter(
        lax.dot_general(
            normalized_signal,
            grad_both,
            (((1,), (1,)), ((), ())),
            preferred_element_type=jnp.float32,
        ),
        "seq",
        scatter_dimension=0,
        tiled=True,
    )
    grad_value = weight_sums[:, :local_cols]
    grad_gate = weight_sums[:, local_cols:]
    normed_term = jnp.dot(gathered, grad_both, preferred_element_type=jnp.float32)
    normalized_gradient = lax.psum_scatter(
        normed_term.astype(jnp.bfloat16), "ch", scatter_dimension=1, tiled=True
    ).astype(jnp.float32)
    scaled_signal = normalized_gradient * complete_gain[:, None]
    first_moment = jnp.mean(scaled_signal, 0, keepdims=True)
    second_moment = jnp.mean(scaled_signal * centered_unit_rows, 0, keepdims=True)
    gradient_rows = (
        row_inverse_deviation * (scaled_signal - first_moment - centered_unit_rows * second_moment)
    ).astype(jnp.bfloat16)
    signal_gradient = lax.all_to_all(gradient_rows, "ch", split_axis=0, concat_axis=1, tiled=True)
    gain_portion = jnp.sum(normalized_gradient * centered_unit_rows, 1)
    gain_whole = lax.psum(gain_portion, ("seq", "ch"))
    gain_gradient = lax.dynamic_slice_in_dim(
        gain_whole, channel_position * local_cols, local_cols, 0
    )
    return (output, signal_gradient, grad_value, grad_gate, grad_taps, gain_gradient)


def solution(mesh):
    placed = (
        P("ch", "seq"),
        P("ch"),
        P("seq", "ch"),
        P("seq", "ch"),
        P(None, "ch"),
        P("ch", "seq"),
    )
    return jax.shard_map(
        shards,
        mesh=mesh,
        in_specs=placed,
        out_specs=(
            P("ch", "seq"),
            P("ch", "seq"),
            P("seq", "ch"),
            P("seq", "ch"),
            P(None, "ch"),
            P("ch"),
        ),
        check_vma=False,
    )
```

profile of v0, /device:TPU:1, one launch (start us, length us, event | category | flops | bytes accessed | tf_op | source)
XLA Modules:
  0.0 592.0 jit_solution(6644750311934210366)
XLA Ops:
  8.0 1.4 pad_maximum_fusion.4
  12.3 20.2 %all-reduce = bf16[1536]{0:T(1024)(128)(2,1)S(1)} all-reduce(bf16[1536]{0:T(1024)(128)(2,1)S(1)} %dynamic-update-slice), channel_id=1, replica_groups=mesh['seq'=64,'ch'=8] {'ch'}, use_global_device_ids=true, to_apply=%add | all-reduce | flops 1536 | bytes 6144
  32.6 22.6 %all-gather.5.cloned.1.call-done = bf16[1536,512]{1,0:T(8,128)(2,1)} async-done(((bf16[192,512]{1,0:T(8,128)(2,1)}), bf16[1536,512]{1,0:T(8,128)(2,1)}) %all-gather.5.cloned.1.call-update) | async-done | bytes 1572880 | tf_op jit(solution)/shard_map/all_gather | solution.py:55
  55.2 1.7 copy.41
  57.8 85.3 %all-gather.3.cloned.1.call-done = bf16[1536,384]{1,0:T(8,128)(2,1)} async-done(((bf16[24,384]{1,0:T(8,128)(2,1)}), bf16[1536,384]{1,0:T(8,128)(2,1)}) %all-gather.3.cloned.1.call-update) | async-done | bytes 1179664 | tf_op jit(solution)/shard_map/all_gather | solution.py:69
  143.1 2.2 fusion.6
  145.6 2.1 collective-permute-start.1
  147.7 3.4 collective-permute-start
  154.1 2.0 convolution_select_fusion.1
  156.1 1.4 copy.58
  158.5 2.0 multiply_convert_fusion.5
  160.6 1.9 collective-permute-start.3
  162.5 4.2 collective-permute-start.2
  168.9 2.0 convolution_select_fusion
  171.0 1.4 copy.59
  174.6 3.5 convolution_convert_fusion
  180.4 2.1 fusion
  183.8 2.7 fusion.5
  186.5 38.9 %reduce-scatter.2.cloned.1.call-done = bf16[1536,64]{0,1:T(8,128)(2,1)} async-done(((bf16[1536,512]{0,1:T(8,128)(2,1)}), bf16[1536,64]{0,1:T(8,128)(2,1)}) %reduce-scatter.2.cloned.1.call-update) | async-done | bytes 196624 | tf_op jit(solution)/shard_map/reduce_scatter | solution.py:107
  228.9 4.7 all-to-all-start
  233.6 2.2 fusion.49
  235.9 245.9 %psum.14 = f32[31,192]{1,0:T(8,128)} all-reduce(f32[31,192]{1,0:T(8,128)S(1)} %bitcast.60), channel_id=1, replica_groups=mesh['seq'=64,'ch'=8] {'seq'}, use_global_device_ids=true, to_apply=%region_6.0 | all-reduce | flops 5952 | bytes 47616 | tf_op jit(solution)/shard_map/psum | solution.py:89
  481.8 1.5 fusion.46
  483.3 100.8 %psum.15 = f32[1536]{0:T(1024)S(1)} all-reduce(f32[1536]{0:T(1024)S(1)} %get-tuple-element.18), channel_id=1, replica_groups=mesh['seq'=64,'ch'=8] {'seq','ch'}, use_global_device_ids=true, to_apply=%region_8.0 | all-reduce | flops 1536 | bytes 12288 | tf_op jit(solution)/shard_map/psum | solution.py:118
  (57 shorter events, 20.3 us)
Async XLA Ops:
  7.2 146.9 %copy-start = (f32[31,192]{1,0:T(8,128)S(1)}, f32[31,192]{1,0:T(8,128)}, u32[]{:S(2)}) copy-start(f32[31,192]{1,0:T(8,128)} %param.10) | copy-start | bytes 71428
  7.2 48.0 %all-gather.5.cloned.1.call-start = ((), (), s32[]{:S(2)}) async-start(), calls=%async_computation.3 | async-start | bytes 1769472 | tf_op jit(solution)/shard_map/all_gather | solution.py:55
  7.9 135.2 %all-gather.3.cloned.1.call-start = ((), (), s32[]{:S(2)}) async-start(), calls=%async_computation.2 | async-start | bytes 1198080 | tf_op jit(solution)/shard_map/all_gather | solution.py:69
  9.4 216.0 %reduce-scatter.2.cloned.1.call-start = ((), (), s32[]{:S(2)}) async-start(), calls=%async_computation.4 | async-start | bytes 1769472 | tf_op jit(solution)/shard_map/reduce_scatter | solution.py:107
  145.3 8.7 %copy-start.2 = (pred[8,68]{0,1:T(8,128)(4,1)S(1)}, pred[8,68]{0,1:T(8,128)(4,1)}, u32[]{:S(2)}) copy-start(pred[8,68]{0,1:T(8,128)(4,1)} %constant.43) | copy-start | bytes 1636
  145.6 5.6 collective-permute-start.1
  147.7 4.6 collective-permute-start
  160.6 6.2 %collective-permute-start.3 = (bf16[192,15]{1,0:T(8,128)(2,1)S(1)}, bf16[192,15]{1,0:T(8,128)(2,1)S(1)}, u32[]{:S(2)}, u32[]{:S(2)}) collective-permute-start(bf16[192,15]{1,0:T(8,128)(2,1)S(1)} %get-tuple-element.30), channel_id=1, source_target_pairs={{8,0},{16,8},{24,16},{32,24},{40,32},{48,40},{56,48},{64,56},{72,6... | collective-permute-start | bytes 17288 | tf_op jit(solution)/shard_map/ppermute | solution.py:17
  162.5 5.4 collective-permute-start.2
  178.1 4.3 copy-start.1
  178.1 303.6 %all-reduce.4.cloned.1.call-start = ((), (), s32[]{:S(2)}) async-start(), calls=%async_computation.5 | async-start | bytes 4718592
  228.9 355.8 %all-to-all-start = ((bf16[8,192,64]{1,2,0:T(8,128)(2,1)}), bf16[8,192,64]{1,2,0:T(8,128)(2,1)S(1)}, u32[]{:S(2)}, u32[]{:S(2)}) async-start(bf16[8,192,64]{1,2,0:T(8,128)(2,1)} %copy.54), calls=%async_computation.1 | async-start | bytes 524288 | tf_op jit(solution)/shard_map/all_to_all | solution.py:116
Sparse Core Ops, SparseCore 0:
  10.1 45.0 all-gather.4
  59.0 84.0 all-gather.2
  178.3 47.0 reduce-scatter.1
  228.6 202.0 all-reduce.3
where the time goes:
time: 593 us; the launch traced here: 592 us
  blocking collectives  367 us (62%)
  waiting for transfers between devices  150 us (25%)
  starting transfers between devices  16.8 us (3%)
  local copies, waits for them, and re-layouts  16.6 us (3%)
  between operations  15.3 us (3%)
  matrix products  14.7 us (2%)
  other arithmetic  11.8 us (2%)
    psum x1, blocking collectives, shards(): grad_taps = lax.psum(tap_partial, 'seq')  246 us
    psum x1, blocking collectives, shards(): gain_whole = lax.psum(gain_portion, ('seq', 'ch'))  101 us
    all_gather x1, waiting for transfers between devices, shards(): gathered = lax.all_gather(stacked, 'seq', axis=0, tiled=True)  85.3 us
    reduce_scatter x1, waiting for transfers between devices, shards(): lax.psum_scatter(normed_term.astype(jnp.bfloat16), 'ch', scatter_dimensio...  38.9 us
    all_gather x1, waiting for transfers between devices, shards(): lax.all_gather(signal, 'ch', axis=0, tiled=True)  22.6 us
    unnamed x1, blocking collectives  20.2 us
  transfers between devices with their start and end apart: 9, of which 5 were waited for; matrix products, arithmetic and copies ran while one was open for 4% of the time, Pallas kernels for 0%

commit v1 on v0

--- a/solution.py
+++ b/solution.py
@@ -1,7 +1,17 @@
+import functools
 import jax
 import jax.numpy as jnp
 from jax import lax
 from jax.sharding import PartitionSpec as P
+
+
+def press_views(in_array, group_axis):
+    o_now = lax.all_gather(in_array, group_axis)
+    inter = jnp.sum(o_now, axis=0)
+    return inter
+
+
+column_test = functools.partial(press_views, group_axis="seq")
 
 
 def extended(cells, sides, width):
@@ -86,7 +96,7 @@
     grad_pad = extended(grad_pre, (("seq", 1),), reach).astype(jnp.float32)
     grad_glued = depthwise(grad_pad, forward_kernel[:, :, ::-1])
     tap_partial = depthwise(glued_pad, grad_pre_f[:, None, :]).T
-    grad_taps = lax.psum(tap_partial, "seq")
+    grad_taps = column_test(tap_partial)
     grad_v = (grad_glued * sig_gate).astype(jnp.bfloat16)
     grad_g = (grad_glued * value * sig_gate * (1.0 - sig_gate)).astype(jnp.bfloat16)
     grad_both = jnp.concatenate([grad_v, grad_g], 0)

time: 593 us -> 626 us (1.056)
  waiting for transfers between devices: 150 us -> 429 us
  blocking collectives: 367 us -> 117 us
    psum x1 -> x0, blocking collectives: 246 us -> none  [shards(): grad_taps = lax.psum(tap_partial, 'seq')]
    unnamed x5 -> x6, waiting for transfers between devices: 0.73 us -> 195 us
    all_gather x0 -> x1, waiting for transfers between devices: none -> 86 us  [press_views(): o_now = lax.all_gather(in_array, group_axis)]
  transfers between devices with their start and end apart: 9 -> 10, of which waited for: 5 -> 7; matrix products, arithmetic and copies ran while one was open for 4% -> 4% of each run, Pallas kernels for 0% -> 0%
where the time goes in v1:
time: 626 us; the launch traced here: 625 us
  waiting for transfers between devices  429 us (69%)
  blocking collectives  117 us (19%)
  local copies, waits for them, and re-layouts  17.2 us (3%)
  starting transfers between devices  16.9 us (3%)
  between operations  15.4 us (2%)
  matrix products  14.6 us (2%)
  other arithmetic  14.1 us (2%)
    unnamed x6, waiting for transfers between devices  195 us
    psum x1, blocking collectives, shards(): gain_whole = lax.psum(gain_portion, ('seq', 'ch'))  97.2 us
    all_gather x1, waiting for transfers between devices, press_views(): o_now = lax.all_gather(in_array, group_axis)  86 us
    all_gather x1, waiting for transfers between devices, shards(): gathered = lax.all_gather(stacked, 'seq', axis=0, tiled=True)  85.3 us
    reduce_scatter x1, waiting for transfers between devices, shards(): lax.psum_scatter(normed_term.astype(jnp.bfloat16), 'ch', scatter_dimensio...  37.9 us
    all_gather x1, waiting for transfers between devices, shards(): lax.all_gather(signal, 'ch', axis=0, tiled=True)  22.6 us
    unnamed x1, blocking collectives  20.2 us
  transfers between devices with their start and end apart: 10, of which 7 were waited for; matrix products, arithmetic and copies ran while one was open for 4% of the time, Pallas kernels for 0%

profile of v1, /device:TPU:1, one launch (start us, length us, event | category | flops | bytes accessed | tf_op | source)
XLA Modules:
  0.0 625.0 jit_solution(15685283141256608414)
XLA Ops:
  12.3 20.2 %all-reduce = bf16[1536]{0:T(1024)(128)(2,1)S(1)} all-reduce(bf16[1536]{0:T(1024)(128)(2,1)S(1)} %dynamic-update-slice), channel_id=1, replica_groups=mesh['seq'=64,'ch'=8] {'ch'}, use_global_device_ids=true, to_apply=%add | all-reduce | flops 1536 | bytes 6144
  32.6 22.6 %all-gather.8.cloned.1.call-done = bf16[1536,512]{1,0:T(8,128)(2,1)} async-done(((bf16[192,512]{1,0:T(8,128)(2,1)}), bf16[1536,512]{1,0:T(8,128)(2,1)}) %all-gather.8.cloned.1.call-update) | async-done | bytes 1572880 | tf_op jit(solution)/shard_map/all_gather | solution.py:65
  55.2 1.7 copy.41
  57.8 85.3 %all-gather.6.cloned.1.call-done = bf16[1536,384]{1,0:T(8,128)(2,1)} async-done(((bf16[24,384]{1,0:T(8,128)(2,1)}), bf16[1536,384]{1,0:T(8,128)(2,1)}) %all-gather.6.cloned.1.call-update) | async-done | bytes 1179664 | tf_op jit(solution)/shard_map/all_gather | solution.py:79
  143.1 2.2 fusion.6
  145.6 2.2 collective-permute-start.1
  147.7 3.4 collective-permute-start
  154.0 2.0 convolution_select_fusion.1
  156.1 1.4 copy.58
  158.5 2.0 multiply_convert_fusion.5
  160.6 1.9 collective-permute-start.3
  162.5 4.2 collective-permute-start.2
  169.0 2.0 convolution_select_fusion
  174.6 3.5 convolution_convert_fusion
  178.1 2.7 fusion.5
  182.4 2.2 fusion.49
  185.4 2.0 fusion
  187.4 37.9 %reduce-scatter.2.cloned.1.call-done = bf16[1536,64]{0,1:T(8,128)(2,1)} async-done(((bf16[1536,512]{0,1:T(8,128)(2,1)}), bf16[1536,64]{0,1:T(8,128)(2,1)}) %reduce-scatter.2.cloned.1.call-update) | async-done | bytes 196624 | tf_op jit(solution)/shard_map/reduce_scatter | solution.py:117
  228.8 4.7 all-to-all-start
  235.5 194.4 %all-reduce.4.cloned.1.call-done = f32[1536,384]{1,0:T(8,128)} async-done(((f32[1536,384]{1,0:T(8,128)}), f32[1536,384]{1,0:T(8,128)}) %all-reduce.4.cloned.1.call-update) | async-done | bytes 2359312
  429.9 1.5 fusion.46
  431.4 86.0 %all-gather.10.cloned.1.call-done = f32[64,31,192]{2,1,0:T(8,128)} async-done(((f32[1,31,192]{2,1,0:T(8,128)}), f32[64,31,192]{2,1,0:T(8,128)}) %all-gather.10.cloned.1.call-update) | async-done | bytes 1523728 | tf_op jit(solution)/shard_map/all_gather | solution.py:9
  517.4 2.4 reduce_sum.58
  519.8 97.2 %psum.7 = f32[1536]{0:T(1024)S(1)} all-reduce(f32[1536]{0:T(1024)S(1)} %get-tuple-element.18), channel_id=1, replica_groups=mesh['seq'=64,'ch'=8] {'seq','ch'}, use_global_device_ids=true, to_apply=%region_8.0 | all-reduce | flops 1536 | bytes 12288 | tf_op jit(solution)/shard_map/psum | solution.py:128
  (60 shorter events, 23.8 us)
Async XLA Ops:
  7.2 146.9 %copy-start = (f32[31,192]{1,0:T(8,128)S(1)}, f32[31,192]{1,0:T(8,128)}, u32[]{:S(2)}) copy-start(f32[31,192]{1,0:T(8,128)} %param.10) | copy-start | bytes 71428
  7.2 48.0 %all-gather.8.cloned.1.call-start = ((), (), s32[]{:S(2)}) async-start(), calls=%async_computation.3 | async-start | bytes 1769472 | tf_op jit(solution)/shard_map/all_gather | solution.py:65
  7.9 135.2 %all-gather.6.cloned.1.call-start = ((), (), s32[]{:S(2)}) async-start(), calls=%async_computation.2 | async-start | bytes 1198080 | tf_op jit(solution)/shard_map/all_gather | solution.py:79
  9.4 215.9 %reduce-scatter.2.cloned.1.call-start = ((), (), s32[]{:S(2)}) async-start(), calls=%async_computation.4 | async-start | bytes 1769472 | tf_op jit(solution)/shard_map/reduce_scatter | solution.py:117
  145.3 8.7 %copy-start.2 = (pred[8,68]{0,1:T(8,128)(4,1)S(1)}, pred[8,68]{0,1:T(8,128)(4,1)}, u32[]{:S(2)}) copy-start(pred[8,68]{0,1:T(8,128)(4,1)} %constant.43) | copy-start | bytes 1636
  145.6 5.6 collective-permute-start.1
  147.7 4.6 collective-permute-start
  160.6 6.2 collective-permute-start.3
  162.5 5.4 collective-permute-start.2
  178.1 3.0 copy-start.1
  178.1 251.8 %all-reduce.4.cloned.1.call-start = ((), (), s32[]{:S(2)}) async-start(), calls=%async_computation.6 | async-start | bytes 4718592
  180.8 336.6 %all-gather.10.cloned.1.call-start = ((), (), s32[]{:S(2)}) async-start(), calls=%async_computation.5 | async-start | bytes 2129920 | tf_op jit(solution)/shard_map/all_gather | solution.py:9
  228.8 388.8 %all-to-all-start = ((bf16[8,192,64]{1,2,0:T(8,128)(2,1)}), bf16[8,192,64]{1,2,0:T(8,128)(2,1)S(1)}, u32[]{:S(2)}, u32[]{:S(2)}) async-start(bf16[8,192,64]{1,2,0:T(8,128)(2,1)} %copy.54), calls=%async_computation.1 | async-start | bytes 524288 | tf_op jit(solution)/shard_map/all_to_all | solution.py:126
Sparse Core Ops, SparseCore 0:
  10.1 45.0 all-gather.7
  59.0 84.0 all-gather.5
  178.2 47.0 reduce-scatter.1
  228.6 201.2 all-reduce.3
  433.7 83.7 all-gather.9
